TPU v7x, 128 devices: a whole 4x4x4 slice. The times are simulated.
128 devices in a mesh: req: 8 (over y, core), voc: 16 (over x, z).
Axes of the slice: x: 4, y: 4, z: 4, core: 2. Of those that a mesh axis runs over, the one named last changes fastest.
Arguments:
- hidden: bfloat16 [16384, 1536], P(('req', 'voc')), may hold values from -64 to 64
- norm_gain: float32 [1536], replicated, may hold values from 0.1 to 1.9
- head: bfloat16 [1536, 49152], P(None, 'voc'), may hold values from -8 to 8
- targets: int32 [16384], P(('req', 'voc')), may hold values from 0 to 49151
- bounds: int32 [128, 2], P(('req', 'voc')), may hold values from 0 to 128, as said below
Outputs:
- logprob: float32 [16384], P(('req', 'voc'))
- entropy: float32 [16384], P(('req', 'voc'))
- target_logit: float32 [16384], P(('req', 'voc'))
- mean_entropy: float32 [1], replicated
Inputs may be any that keep to these rules, and one draw needn't show every extreme that they name: bounds[d] = (lo, hi): slots lo to hi - 1 of device d hold live response rows; 1 <= hi - lo <= 96, lo <= 32; some device has hi - lo = 96 and hi = 128, some has lo = 0.
All inputs are finite; a program needn't handle non-finite values.
Results may differ from a plain program's by a relative error of at most 0.00075.
The roundings to bfloat16 on the way count: a program that leaves them out, or rounds other values in their place, can miss the bound.
Values may be sent and summed in bfloat16 or wider, within the bound.
No kernel may reach another device: no remote copies, remote signals or barrier semaphores. Data moves between devices by JAX's collectives and lax.ppermute only.
A program may use at most 64 MiB of HBM per device.

v0:
```python
import jax
import jax.numpy as jnp
from jax import lax
from jax.sharding import PartitionSpec as P

LIVE = 96
CHUNK = 32


def pick_block(count):
    size = min(count, 512)
    while count % size:
        size -= 1
    return size


def combine_stats(first, second):
    top = jnp.maximum(first[0], second[0])
    weight_a = jnp.exp(first[0] - top)
    weight_b = jnp.exp(second[0] - top)
    return jnp.stack(
        [
            top,
            first[1] * weight_a + second[1] * weight_b,
            first[2] * weight_a + second[2] * weight_b,
            first[3] + second[3],
        ]
    )


def butterfly(value, axis, combine):
    size = lax.axis_size(axis)
    index = lax.axis_index(axis)
    step = 1
    while step < size:
        other = lax.ppermute(value, axis, [(i, i ^ step) for i in range(size)])
        upper = index & step != 0
        first = jnp.where(upper, other, value)
        second = jnp.where(upper, value, other)
        value = combine(first, second)
        step *= 2
    return value


def members(value, axis, sub, stride):
    size = lax.axis_size(axis)
    digit = lax.axis_index(axis) // stride % sub
    received = [value]
    for shift in range(1, sub):
        pairs = []
        for i in range(size):
            d = i // stride % sub
            pairs.append((i, i + ((d + shift) % sub - d) * stride))
        received.append(lax.ppermute(value, axis, pairs))
    order = (digit - jnp.arange(sub, dtype=jnp.int32)) % sub
    return jnp.take(jnp.stack(received), order, axis=0)


def tree(items, combine):
    items = list(items)
    while len(items) > 1:
        items = [combine(items[i], items[i + 1]) for i in range(0, len(items), 2)]
    return items[0]


def shard_stats(gathered, local_ids, head):
    count = gathered.shape[0]
    width = gathered.shape[1]
    block = pick_block(count)
    columns = jnp.arange(head.shape[1], dtype=jnp.int32)

    def one_block(pair):
        rows_in, ids = pair
        logits = jnp.dot(rows_in, head, preferred_element_type=jnp.float32)
        top = jnp.max(logits, axis=-1)
        expo = jnp.exp(logits - top[:, None])
        total = jnp.sum(expo, axis=-1)
        weighted = jnp.sum(expo * logits, axis=-1)
        picked = jnp.sum(jnp.where(columns[None, :] == ids[:, None], logits, 0.0), axis=-1)
        return jnp.stack([top, total, weighted, picked])

    outputs = lax.map(
        one_block,
        (gathered.reshape(count // block, block, width), local_ids.reshape(count // block, block)),
    )
    return jnp.transpose(outputs, (1, 0, 2)).reshape(4, count)


def shards(hidden, norm_gain, head, targets, bounds):
    slots = hidden.shape[0]
    shard_width = head.shape[1]
    groups = lax.axis_size("voc")
    position = lax.axis_index("voc")
    start = bounds[0, 0]
    finish = bounds[0, 1]
    live_count = finish - start
    rows = lax.dynamic_slice_in_dim(hidden, start, LIVE, 0)
    values = rows.astype(jnp.float32)
    meansq = jnp.mean(values * values, axis=-1, keepdims=True)
    normed = (values * lax.rsqrt(meansq + 1e-05) * norm_gain).astype(jnp.bfloat16)
    ids = lax.dynamic_slice_in_dim(targets, start, LIVE, 0)
    meta = jnp.concatenate([ids, jnp.full((8,), live_count, jnp.int32)])
    gathered_meta = lax.all_gather(meta, "voc", axis=0)
    gathered_ids = gathered_meta[:, :LIVE]
    counts = gathered_meta[:, LIVE]
    local_ids = gathered_ids - position * shard_width
    parts = []
    for first in range(0, LIVE, CHUNK):
        gathered = lax.all_gather(normed[first : first + CHUNK], "voc", axis=0, tiled=True)
        part = shard_stats(gathered, local_ids[:, first : first + CHUNK].reshape(-1), head)
        parts.append(part.reshape(4, groups, CHUNK))
    stats = jnp.stack(parts, axis=2).reshape(4, groups * LIVE)
    inner = 4 if groups % 4 == 0 else 1
    merged = stats
    if inner > 1:
        merged = tree(members(merged, "voc", inner, 1), combine_stats)
    merged = tree(members(merged, "voc", groups // inner, inner), combine_stats)
    top, total, weighted, picked = (merged[0], merged[1], merged[2], merged[3])
    lse = top + jnp.log(total)
    row_entropy = lse - weighted / total
    row_logprob = picked - lse
    slot = jnp.arange(LIVE, dtype=jnp.int32)
    group_live = slot[None, :] < counts[:, None]
    group_entropy = jnp.where(group_live, row_entropy.reshape(groups, LIVE), 0.0)
    totals = jnp.stack([jnp.sum(group_entropy), jnp.sum(counts).astype(jnp.float32)])
    totals = tree(members(totals, "req", lax.axis_size("req"), 1), lambda a, b: a + b)
    mean_entropy = (totals[0] / totals[1]).reshape(1)
    own = lambda a: lax.dynamic_slice_in_dim(a, position * LIVE, LIVE, 0)
    live = slot < live_count
    zero = jnp.zeros((LIVE,), jnp.float32)
    place = lambda a: lax.dynamic_update_slice_in_dim(jnp.zeros((slots,), jnp.float32), a, start, 0)
    entropy = place(jnp.where(live, own(row_entropy), zero))
    logprob = place(jnp.where(live, own(row_logprob), zero))
    target_logit = place(jnp.where(live, own(picked), zero))
    return (logprob, entropy, target_logit, mean_entropy)


def solution(mesh):
    placed = (
        P(("req", "voc"), None),
        P(),
        P(None, "voc"),
        P(("req", "voc")),
        P(("req", "voc"), None),
    )
    return jax.shard_map(
        shards,
        mesh=mesh,
        in_specs=placed,
        out_specs=(P(("req", "voc")), P(("req", "voc")), P(("req", "voc")), P()),
        check_vma=False,
    )
```

profile of v0, /device:TPU:1, one launch (start us, length us, event | category | flops | bytes accessed | tf_op | source)
XLA Modules:
  0.0 206.2 jit_solution(10489201134984408602)
XLA Ops:
  7.2 1.3 fusion.51
  10.5 1.2 fusion.3
  17.1 1.2 dynamic-slice.4
  19.1 14.9 %all-reduce.1 = s32[1664]{0:T(1024)S(1)} all-reduce(s32[1664]{0:T(1024)S(1)} %pad_dynamic-update-slice_fusion), channel_id=2, replica_groups=mesh['req'=8,'voc'=16] {'voc'}, use_global_device_ids=true, to_apply=%add.1 | all-reduce | flops 1664 | bytes 13312
  35.3 24.1 %all-gather.5.cloned.1.call-done = bf16[512,1536]{1,0:T(8,128)(2,1)} async-done(((bf16[32,1536]{1,0:T(8,128)(2,1)}), bf16[512,1536]{1,0:T(8,128)(2,1)}) %all-gather.5.cloned.1.call-update) | async-done | bytes 1572880 | tf_op jit(solution)/shard_map/all_gather | solution.py:109
  59.5 9.8 %fusion.54 = (f32[512]{0:T(512)S(1)}, f32[512,3072]{1,0:T(8,128)}) fusion(bf16[512,1536]{1,0:T(8,128)(2,1)} %all-gather.5.cloned.1.call-done, bf16[1536,3072]{1,0:T(8,128)(2,1)} %param.9), kind=kOutput, calls=%fused_computation.162 | convolution fusion | flops 4833410560 | bytes 17303552 | tf_op jit(solution)/shard_map/while/body/eval_jaxpr/dot_general | solution.py:74
  69.4 4.6 %fusion.2 = (f32[512]{0:T(512)S(1)}, f32[512]{0:T(512)S(1)}, f32[512]{0:T(512)S(1)}) fusion(f32[512,3072]{1,0:T(8,128)} %get-tuple-element.117, f32[512]{0:T(512)S(1)} %get-tuple-element.116, s32[512]{0:T(512)S(1)} %eq.76), kind=kLoop, calls=%fused_computation.17 | loop fusion | flops 11008512 | bytes 6301696 | tf_op jit(solution)/shard_map/while/body/eval_jaxpr/reduce_sum | solution.py:77
  74.3 30.5 %all-gather.7.cloned.1.call-done = bf16[512,1536]{1,0:T(8,128)(2,1)} async-done(((bf16[32,1536]{1,0:T(8,128)(2,1)}), bf16[512,1536]{1,0:T(8,128)(2,1)}) %all-gather.7.cloned.1.call-update) | async-done | bytes 1572880 | tf_op jit(solution)/shard_map/all_gather | solution.py:109
  104.8 9.8 %fusion.53 = (f32[512]{0:T(512)S(1)}, f32[512,3072]{1,0:T(8,128)}) fusion(bf16[512,1536]{1,0:T(8,128)(2,1)} %all-gather.7.cloned.1.call-done, bf16[1536,3072]{1,0:T(8,128)(2,1)} %param.9), kind=kOutput, calls=%fused_computation.161 | convolution fusion | flops 4833410560 | bytes 17303552 | tf_op jit(solution)/shard_map/while/body/eval_jaxpr/dot_general | solution.py:74
  114.7 4.6 %fusion.1 = (f32[512]{0:T(512)S(1)}, f32[512]{0:T(512)S(1)}, f32[512]{0:T(512)S(1)}) fusion(f32[512,3072]{1,0:T(8,128)} %get-tuple-element.115, f32[512]{0:T(512)S(1)} %get-tuple-element.114, s32[512]{0:T(512)S(1)} %eq.80), kind=kLoop, calls=%fused_computation.12 | loop fusion | flops 11008512 | bytes 6301696 | tf_op jit(solution)/shard_map/while/body/eval_jaxpr/reduce_sum | solution.py:77
  119.6 30.5 %all-gather.9.cloned.1.call-done = bf16[512,1536]{1,0:T(8,128)(2,1)} async-done(((bf16[32,1536]{1,0:T(8,128)(2,1)}), bf16[512,1536]{1,0:T(8,128)(2,1)}) %all-gather.9.cloned.1.call-update) | async-done | bytes 1572880 | tf_op jit(solution)/shard_map/all_gather | solution.py:109
  150.0 9.8 %fusion.52 = (f32[512]{0:T(512)S(1)}, f32[512,3072]{1,0:T(8,128)}) fusion(bf16[512,1536]{1,0:T(8,128)(2,1)} %all-gather.9.cloned.1.call-done, bf16[1536,3072]{1,0:T(8,128)(2,1)} %param.9), kind=kOutput, calls=%fused_computation.160 | convolution fusion | flops 4833410560 | bytes 17303552 | tf_op jit(solution)/shard_map/while/body/eval_jaxpr/dot_general | solution.py:74
  160.0 4.6 %fusion = (f32[512]{0:T(512)S(1)}, f32[512]{0:T(512)S(1)}, f32[512]{0:T(512)S(1)}) fusion(f32[512,3072]{1,0:T(8,128)} %get-tuple-element.113, f32[512]{0:T(512)S(1)} %get-tuple-element.112, s32[512]{0:T(512)S(1)} %eq.84), kind=kLoop, calls=%fused_computation.7 | loop fusion | flops 11008512 | bytes 6301696 | tf_op jit(solution)/shard_map/while/body/eval_jaxpr/reduce_sum | solution.py:77
  166.1 2.4 %collective-permute-start.1 = (f32[4,1536]{1,0:T(4,128)S(1)}, f32[4,1536]{1,0:T(4,128)S(1)}, u32[]{:S(2)}, u32[]{:S(2)}) collective-permute-start(f32[4,1536]{1,0:T(4,128)S(1)} %reshape.534), channel_id=1, source_target_pairs={{0,2},{1,3},{2,0},{3,1},{4,6},{5,7},{6,4},{7,5},{8,10},{9,11},{10,... | collective-permute-start | bytes 73736 | tf_op jit(solution)/shard_map/ppermute | solution.py:54
  169.1 1.2 collective-permute-done.1
  170.3 1.2 collective-permute-done.2
  172.5 1.8 collective-permute-start.4
  174.2 1.2 collective-permute-start.5
  179.5 5.9 %collective-permute-start.6 = (f32[2]{0:T(128)S(1)}, f32[2]{0:T(128)S(1)}, u32[]{:S(2)}, u32[]{:S(2)}) collective-permute-start(f32[2]{0:T(128)S(1)} %pad_maximum_fusion.3), channel_id=1, source_target_pairs={{0,16},{16,32},{32,48},{48,64},{64,80},{80,96},{96,112},{112,0},{1... | collective-permute-start | bytes 32 | tf_op jit(solution)/shard_map/ppermute | solution.py:54
  185.4 1.2 collective-permute-start.7
  186.6 1.5 collective-permute-start.8
  188.6 2.0 collective-permute-start.10
  192.8 1.6 collective-permute-start.12
  194.6 1.3 collective-permute-done.12
  (92 shorter events, 16.7 us)
Async XLA Ops:
  7.2 52.3 %all-gather.5.cloned.1.call-start = ((), (), s32[]{:S(2)}) async-start(), calls=%async_computation | async-start | bytes 1671168 | tf_op jit(solution)/shard_map/all_gather | solution.py:109
  13.5 91.2 %all-gather.7.cloned.1.call-start = ((), (), s32[]{:S(2)}) async-start(), calls=%async_computation.1 | async-start | bytes 1671168 | tf_op jit(solution)/shard_map/all_gather | solution.py:109
  14.3 135.8 %all-gather.9.cloned.1.call-start = ((), (), s32[]{:S(2)}) async-start(), calls=%async_computation.2 | async-start | bytes 1671168 | tf_op jit(solution)/shard_map/all_gather | solution.py:109
  165.1 4.0 %collective-permute-start = (f32[4,1536]{1,0:T(4,128)S(1)}, f32[4,1536]{1,0:T(4,128)S(1)}, u32[]{:S(2)}, u32[]{:S(2)}) collective-permute-start(f32[4,1536]{1,0:T(4,128)S(1)} %reshape.534), channel_id=1, source_target_pairs={{0,1},{1,2},{2,3},{3,0},{4,5},{5,6},{6,7},{7,4},{8,9},{9,10},{10,1... | collective-permute-start | bytes 73736 | tf_op jit(solution)/shard_map/ppermute | solution.py:54
  166.1 4.2 %collective-permute-start.1 = (f32[4,1536]{1,0:T(4,128)S(1)}, f32[4,1536]{1,0:T(4,128)S(1)}, u32[]{:S(2)}, u32[]{:S(2)}) collective-permute-start(f32[4,1536]{1,0:T(4,128)S(1)} %reshape.534), channel_id=1, source_target_pairs={{0,2},{1,3},{2,0},{3,1},{4,6},{5,7},{6,4},{7,5},{8,10},{9,11},{10,... | collective-permute-start | bytes 73736 | tf_op jit(solution)/shard_map/ppermute | solution.py:54
  168.5 3.0 %collective-permute-start.2 = (f32[4,1536]{1,0:T(4,128)S(1)}, f32[4,1536]{1,0:T(4,128)S(1)}, u32[]{:S(2)}, u32[]{:S(2)}) collective-permute-start(f32[4,1536]{1,0:T(4,128)S(1)} %reshape.534), channel_id=1, source_target_pairs={{0,3},{1,0},{2,1},{3,2},{4,7},{5,4},{6,5},{7,6},{8,11},{9,8},{10,9... | collective-permute-start | bytes 73736 | tf_op jit(solution)/shard_map/ppermute | solution.py:54
  172.4 4.0 %collective-permute-start.3 = (f32[4,1536]{1,0:T(4,128)S(1)}, f32[4,1536]{1,0:T(4,128)S(1)}, u32[]{:S(2)}, u32[]{:S(2)}) collective-permute-start(f32[4,1536]{1,0:T(4,128)S(1)} %get-tuple-element.104), channel_id=1, source_target_pairs={{0,4},{1,5},{2,6},{3,7},{4,8},{5,9},{6,10},{7,11},{8,12},{9,13},{1... | collective-permute-start | bytes 73736 | tf_op jit(solution)/shard_map/ppermute | solution.py:54
  172.5 4.4 %collective-permute-start.4 = (f32[4,1536]{1,0:T(4,128)S(1)}, f32[4,1536]{1,0:T(4,128)S(1)}, u32[]{:S(2)}, u32[]{:S(2)}) collective-permute-start(f32[4,1536]{1,0:T(4,128)S(1)} %get-tuple-element.104), channel_id=1, source_target_pairs={{0,8},{1,9},{2,10},{3,11},{4,12},{5,13},{6,14},{7,15},{8,0},{9,1},... | collective-permute-start | bytes 73736 | tf_op jit(solution)/shard_map/ppermute | solution.py:54
  174.2 3.0 %collective-permute-start.5 = (f32[4,1536]{1,0:T(4,128)S(1)}, f32[4,1536]{1,0:T(4,128)S(1)}, u32[]{:S(2)}, u32[]{:S(2)}) collective-permute-start(f32[4,1536]{1,0:T(4,128)S(1)} %get-tuple-element.104), channel_id=1, source_target_pairs={{0,12},{1,13},{2,14},{3,15},{4,0},{5,1},{6,2},{7,3},{8,4},{9,5},{1... | collective-permute-start | bytes 73736 | tf_op jit(solution)/shard_map/ppermute | solution.py:54
  179.5 12.6 %collective-permute-start.6 = (f32[2]{0:T(128)S(1)}, f32[2]{0:T(128)S(1)}, u32[]{:S(2)}, u32[]{:S(2)}) collective-permute-start(f32[2]{0:T(128)S(1)} %pad_maximum_fusion.3), channel_id=1, source_target_pairs={{0,16},{16,32},{32,48},{48,64},{64,80},{80,96},{96,112},{112,0},{1... | collective-permute-start | bytes 32 | tf_op jit(solution)/shard_map/ppermute | solution.py:54
  185.4 7.4 %collective-permute-start.7 = (f32[2]{0:T(128)S(1)}, f32[2]{0:T(128)S(1)}, u32[]{:S(2)}, u32[]{:S(2)}) collective-permute-start(f32[2]{0:T(128)S(1)} %pad_maximum_fusion.3), channel_id=1, source_target_pairs={{0,32},{16,48},{32,64},{48,80},{64,96},{80,112},{96,0},{112,16},{1... | collective-permute-start | bytes 32 | tf_op jit(solution)/shard_map/ppermute | solution.py:54
  186.6 7.8 %collective-permute-start.8 = (f32[2]{0:T(128)S(1)}, f32[2]{0:T(128)S(1)}, u32[]{:S(2)}, u32[]{:S(2)}) collective-permute-start(f32[2]{0:T(128)S(1)} %pad_maximum_fusion.3), channel_id=1, source_target_pairs={{0,48},{16,64},{32,80},{48,96},{64,112},{80,0},{96,16},{112,32},{1... | collective-permute-start | bytes 32 | tf_op jit(solution)/shard_map/ppermute | solution.py:54
  188.1 6.3 %collective-permute-start.9 = (f32[2]{0:T(128)S(1)}, f32[2]{0:T(128)S(1)}, u32[]{:S(2)}, u32[]{:S(2)}) collective-permute-start(f32[2]{0:T(128)S(1)} %pad_maximum_fusion.3), channel_id=1, source_target_pairs={{0,64},{16,80},{32,96},{48,112},{64,0},{80,16},{96,32},{112,48},{1... | collective-permute-start | bytes 32 | tf_op jit(solution)/shard_map/ppermute | solution.py:54
  188.6 5.8 %collective-permute-start.10 = (f32[2]{0:T(128)S(1)}, f32[2]{0:T(128)S(1)}, u32[]{:S(2)}, u32[]{:S(2)}) collective-permute-start(f32[2]{0:T(128)S(1)} %pad_maximum_fusion.3), channel_id=1, source_target_pairs={{0,80},{16,96},{32,112},{48,0},{64,16},{80,32},{96,48},{112,64},{1... | collective-permute-start | bytes 32 | tf_op jit(solution)/shard_map/ppermute | solution.py:54
  191.7 6.9 %copy-start.1 = (f32[128]{0:T(128)}, f32[128]{0:T(128)S(1)}, u32[]{:S(2)}) copy-start(f32[128]{0:T(128)S(1)} %fusion.41) | copy-start | bytes 1540
  191.9 6.6 %copy-start.2 = (f32[128]{0:T(128)}, f32[128]{0:T(128)S(1)}, u32[]{:S(2)}) copy-start(f32[128]{0:T(128)S(1)} %fusion.40) | copy-start | bytes 1540
  192.1 6.5 %copy-start = (f32[128]{0:T(128)}, f32[128]{0:T(128)S(1)}, u32[]{:S(2)}) copy-start(f32[128]{0:T(128)S(1)} %select_dynamic-update-slice_fusion) | copy-start | bytes 1540
  192.1 2.5 %collective-permute-start.11 = (f32[2]{0:T(128)S(1)}, f32[2]{0:T(128)S(1)}, u32[]{:S(2)}, u32[]{:S(2)}) collective-permute-start(f32[2]{0:T(128)S(1)} %pad_maximum_fusion.3), channel_id=1, source_target_pairs={{0,96},{16,112},{32,0},{48,16},{64,32},{80,48},{96,64},{112,80},{1... | collective-permute-start | bytes 32 | tf_op jit(solution)/shard_map/ppermute | solution.py:54
  192.8 3.1 %collective-permute-start.12 = (f32[2]{0:T(128)S(1)}, f32[2]{0:T(128)S(1)}, u32[]{:S(2)}, u32[]{:S(2)}) collective-permute-start(f32[2]{0:T(128)S(1)} %pad_maximum_fusion.3), channel_id=1, source_target_pairs={{0,112},{16,0},{32,16},{48,32},{64,48},{80,64},{96,80},{112,96},{1... | collective-permute-start | bytes 32 | tf_op jit(solution)/shard_map/ppermute | solution.py:54
Sparse Core Ops, SparseCore 0:
  13.7 45.7 all-gather.4
  61.6 43.0 all-gather.6
  106.9 43.0 all-gather.8
where the time goes:
time: 206 us
  waiting for transfers between devices  91.6 us (44%)
  matrix products  29.5 us (14%)
  between operations  21.1 us (10%)
  other arithmetic  20.5 us (10%)
  starting transfers between devices  20.1 us (10%)
  blocking collectives  14.9 us (7%)
  local copies, waits for them, and re-layouts  8.43 us (4%)
    all_gather x3, waiting for transfers between devices, shards(): lax.all_gather(normed[first:first + CHUNK], 'voc', axis=0, tiled=True)  85.1 us
    dot_general x3, matrix products, one_block(): logits = jnp.dot(rows_in, head, preferred_element_type=jnp.float32)  29.5 us
    ppermute x13, starting transfers between devices, members(): received.append(lax.ppermute(value, axis, pairs))  20 us
    unnamed x1, blocking collectives  14.9 us
    reduce_sum x3, other arithmetic, one_block(): total = jnp.sum(expo, axis=-1)  13.9 us
    ppermute x13, waiting for transfers between devices, members(): received.append(lax.ppermute(value, axis, pairs))  5.17 us
  transfers between devices with their start and end apart: 16, of which 11 were waited for; matrix products, arithmetic and copies ran while one was open for 17% of the time, Pallas kernels for 0%

commit v1 on v0

--- a/solution.py
+++ b/solution.py
@@ -106,7 +106,11 @@
     local_ids = gathered_ids - position * shard_width
     parts = []
     for first in range(0, LIVE, CHUNK):
-        gathered = lax.all_gather(normed[first : first + CHUNK], "voc", axis=0, tiled=True)
+        matrix = normed[first : first + CHUNK]
+        block_now = lax.axis_size("voc")
+        w1 = jnp.stack(block_now * [matrix])
+        b_next = lax.all_to_all(w1, axis_name="voc", split_axis=0, concat_axis=0)
+        gathered = jnp.concatenate(b_next, axis=0)
         part = shard_stats(gathered, local_ids[:, first : first + CHUNK].reshape(-1), head)
         parts.append(part.reshape(4, groups, CHUNK))
     stats = jnp.stack(parts, axis=2).reshape(4, groups * LIVE)

time: 206 us -> 149 us (0.72)
  waiting for transfers between devices: 91.6 us -> 11.6 us
  starting transfers between devices: 20.1 us -> 43.6 us
  between operations: 21.1 us -> 8.01 us
  blocking collectives: 14.9 us -> 21.4 us
  matrix products: 29.5 us -> 32.5 us
    all_gather x3 -> x0, waiting for transfers between devices: 85.1 us -> none  [shards(): lax.all_gather(normed[first:first + CHUNK], 'voc', axis=0, tiled=True)]
    all_to_all x0 -> x3, starting transfers between devices: none -> 21.3 us  [shards(): b_next = lax.all_to_all(w1, axis_name='voc', split_axis=0, concat_axis=0)]
    all_to_all x0 -> x3, waiting for transfers between devices: none -> 7.46 us  [shards(): b_next = lax.all_to_all(w1, axis_name='voc', split_axis=0, concat_axis=0)]
    unnamed x1, blocking collectives: 14.9 us -> 21.4 us
    another operation x3 -> x6, local copies, waits for them, and re-layouts: 0.01 us -> 3.91 us  [the longest x3 3.9 us: shards(): w1 = jnp.stack(block_now * [matrix])]
    dot_general x3, matrix products: 29.5 us -> 32.5 us  [one_block(): logits = jnp.dot(rows_in, head, preferred_element_type=jnp.float32)]
    ppermute x13, starting transfers between devices: 20 us -> 22.3 us  [members(): received.append(lax.ppermute(value, axis, pairs))]
  transfers between devices with their start and end apart: 16 -> 16, of which waited for: 11 -> 7; matrix products, arithmetic and copies ran while one was open for 17% -> 24% of each run, Pallas kernels for 0% -> 0%
where the time goes in v1:
time: 149 us; the launch traced here: 148 us
  starting transfers between devices  43.6 us (29%)
  matrix products  32.5 us (22%)
  blocking collectives  21.4 us (14%)
  other arithmetic  20.5 us (14%)
  waiting for transfers between devices  11.6 us (8%)
  local copies, waits for them, and re-layouts  10.3 us (7%)
  between operations  8.01 us (5%)
    dot_general x3, matrix products, one_block(): logits = jnp.dot(rows_in, head, preferred_element_type=jnp.float32)  32.5 us
    ppermute x13, starting transfers between devices, members(): received.append(lax.ppermute(value, axis, pairs))  22.3 us
    unnamed x1, blocking collectives  21.4 us
    all_to_all x3, starting transfers between devices, shards(): b_next = lax.all_to_all(w1, axis_name='voc', split_axis=0, concat_axis=0)  21.3 us
    reduce_sum x3, other arithmetic, one_block(): total = jnp.sum(expo, axis=-1)  13.9 us
    all_to_all x3, waiting for transfers between devices, shards(): b_next = lax.all_to_all(w1, axis_name='voc', split_axis=0, concat_axis=0)  7.46 us
    ppermute x13, waiting for transfers between devices, members(): received.append(lax.ppermute(value, axis, pairs))  4.17 us
    another operation x3, local copies, waits for them, and re-layouts, shards(): w1 = jnp.stack(block_now * [matrix])  3.9 us
  transfers between devices with their start and end apart: 16, of which 7 were waited for; matrix products, arithmetic and copies ran while one was open for 24% of the time, Pallas kernels for 0%

profile of v1, /device:TPU:1, one launch (start us, length us, event | category | flops | bytes accessed | tf_op | source)
XLA Modules:
  0.0 147.9 jit_solution(6996808744537609206)
XLA Ops:
  0.7 1.3 fusion.51
  6.3 1.3 stack.190
  7.6 8.4 %all-to-all-start = ((bf16[16,32,1536]{2,1,0:T(8,128)(2,1)}), bf16[16,32,1536]{2,1,0:T(8,128)(2,1)S(1)}, u32[]{:S(2)}, u32[]{:S(2)}) async-start(bf16[16,32,1536]{2,1,0:T(8,128)(2,1)} %stack.190), calls=%async_computation | async-start | bytes 3145728 | tf_op jit(solution)/shard_map/all_to_all | solution.py:112
  18.8 21.4 %all-reduce.1 = s32[1664]{0:T(1024)S(1)} all-reduce(s32[1664]{0:T(1024)S(1)} %pad_dynamic-update-slice_fusion), channel_id=2, replica_groups=mesh['req'=8,'voc'=16] {'voc'}, use_global_device_ids=true, to_apply=%add.1 | all-reduce | flops 1664 | bytes 13312
  41.4 1.3 stack.196
  42.7 6.1 %all-to-all-start.1 = ((bf16[16,32,1536]{2,1,0:T(8,128)(2,1)}), bf16[16,32,1536]{2,1,0:T(8,128)(2,1)S(1)}, u32[]{:S(2)}, u32[]{:S(2)}) async-start(bf16[16,32,1536]{2,1,0:T(8,128)(2,1)} %stack.196), calls=%async_computation.1 | async-start | bytes 3145728 | tf_op jit(solution)/shard_map/all_to_all | solution.py:112
  48.9 10.7 %fusion.54 = (f32[512]{0:T(512)S(1)}, f32[512,3072]{1,0:T(8,128)}) fusion(bf16[512,1536]{1,0:T(8,128)(2,1)S(1)} %bitcast.180, bf16[1536,3072]{1,0:T(8,128)(2,1)} %param.9), kind=kOutput, calls=%fused_computation.162 | convolution fusion | flops 4833410560 | bytes 17303552 | tf_op jit(solution)/shard_map/while/body/eval_jaxpr/dot_general | solution.py:74
  59.7 4.6 %fusion.2 = (f32[512]{0:T(512)S(1)}, f32[512]{0:T(512)S(1)}, f32[512]{0:T(512)S(1)}) fusion(f32[512,3072]{1,0:T(8,128)} %get-tuple-element.117, f32[512]{0:T(512)S(1)} %get-tuple-element.116, s32[512]{0:T(512)S(1)} %eq.76), kind=kLoop, calls=%fused_computation.17 | loop fusion | flops 11008512 | bytes 6301696 | tf_op jit(solution)/shard_map/while/body/eval_jaxpr/reduce_sum | solution.py:77
  64.6 3.3 %all-to-all-done.1 = bf16[16,32,1536]{2,1,0:T(8,128)(2,1)S(1)} async-done(((bf16[16,32,1536]{2,1,0:T(8,128)(2,1)}), bf16[16,32,1536]{2,1,0:T(8,128)(2,1)S(1)}, u32[]{:S(2)}, u32[]{:S(2)}) %all-to-all-start.1) | async-done | bytes 1572896 | tf_op jit(solution)/shard_map/all_to_all | solution.py:112
  67.8 1.3 stack.202
  69.1 6.8 %all-to-all-start.2 = ((bf16[16,32,1536]{2,1,0:T(8,128)(2,1)}), bf16[16,32,1536]{2,1,0:T(8,128)(2,1)S(1)}, u32[]{:S(2)}, u32[]{:S(2)}) async-start(bf16[16,32,1536]{2,1,0:T(8,128)(2,1)} %stack.202), calls=%async_computation.2 | async-start | bytes 3145728 | tf_op jit(solution)/shard_map/all_to_all | solution.py:112
  76.0 11.0 %fusion.53 = (f32[512]{0:T(512)S(1)}, f32[512,3072]{1,0:T(8,128)}) fusion(bf16[512,1536]{1,0:T(8,128)(2,1)S(1)} %bitcast.181, bf16[1536,3072]{1,0:T(8,128)(2,1)} %param.9), kind=kOutput, calls=%fused_computation.161 | convolution fusion | flops 4833410560 | bytes 17303552 | tf_op jit(solution)/shard_map/while/body/eval_jaxpr/dot_general | solution.py:74
  87.1 4.6 %fusion.1 = (f32[512]{0:T(512)S(1)}, f32[512]{0:T(512)S(1)}, f32[512]{0:T(512)S(1)}) fusion(f32[512,3072]{1,0:T(8,128)} %get-tuple-element.115, f32[512]{0:T(512)S(1)} %get-tuple-element.114, s32[512]{0:T(512)S(1)} %eq.80), kind=kLoop, calls=%fused_computation.12 | loop fusion | flops 11008512 | bytes 6301696 | tf_op jit(solution)/shard_map/while/body/eval_jaxpr/reduce_sum | solution.py:77
  92.0 4.2 %all-to-all-done.2 = bf16[16,32,1536]{2,1,0:T(8,128)(2,1)S(1)} async-done(((bf16[16,32,1536]{2,1,0:T(8,128)(2,1)}), bf16[16,32,1536]{2,1,0:T(8,128)(2,1)S(1)}, u32[]{:S(2)}, u32[]{:S(2)}) %all-to-all-start.2) | async-done | bytes 1572896 | tf_op jit(solution)/shard_map/all_to_all | solution.py:112
  96.2 10.7 %fusion.52 = (f32[512]{0:T(512)S(1)}, f32[512,3072]{1,0:T(8,128)}) fusion(bf16[512,1536]{1,0:T(8,128)(2,1)S(1)} %bitcast.182, bf16[1536,3072]{1,0:T(8,128)(2,1)} %param.9), kind=kOutput, calls=%fused_computation.160 | convolution fusion | flops 4833410560 | bytes 17303552 | tf_op jit(solution)/shard_map/while/body/eval_jaxpr/dot_general | solution.py:74
  107.0 4.6 %fusion = (f32[512]{0:T(512)S(1)}, f32[512]{0:T(512)S(1)}, f32[512]{0:T(512)S(1)}) fusion(f32[512,3072]{1,0:T(8,128)} %get-tuple-element.113, f32[512]{0:T(512)S(1)} %get-tuple-element.112, s32[512]{0:T(512)S(1)} %eq.84), kind=kLoop, calls=%fused_computation.7 | loop fusion | flops 11008512 | bytes 6301696 | tf_op jit(solution)/shard_map/while/body/eval_jaxpr/reduce_sum | solution.py:77
  112.7 1.7 %collective-permute-start.1 = (f32[4,1536]{1,0:T(4,128)S(1)}, f32[4,1536]{1,0:T(4,128)S(1)}, u32[]{:S(2)}, u32[]{:S(2)}) collective-permute-start(f32[4,1536]{1,0:T(4,128)S(1)} %reshape.534), channel_id=1, source_target_pairs={{0,2},{1,3},{2,0},{3,1},{4,6},{5,7},{6,4},{7,5},{8,10},{9,11},{10,... | collective-permute-start | bytes 73736 | tf_op jit(solution)/shard_map/ppermute | solution.py:54
  118.0 2.2 %collective-permute-start.3 = (f32[4,1536]{1,0:T(4,128)S(1)}, f32[4,1536]{1,0:T(4,128)S(1)}, u32[]{:S(2)}, u32[]{:S(2)}) collective-permute-start(f32[4,1536]{1,0:T(4,128)S(1)} %get-tuple-element.104), channel_id=1, source_target_pairs={{0,4},{1,5},{2,6},{3,7},{4,8},{5,9},{6,10},{7,11},{8,12},{9,13},{1... | collective-permute-start | bytes 73736 | tf_op jit(solution)/shard_map/ppermute | solution.py:54
  120.1 1.5 %collective-permute-start.4 = (f32[4,1536]{1,0:T(4,128)S(1)}, f32[4,1536]{1,0:T(4,128)S(1)}, u32[]{:S(2)}, u32[]{:S(2)}) collective-permute-start(f32[4,1536]{1,0:T(4,128)S(1)} %get-tuple-element.104), channel_id=1, source_target_pairs={{0,8},{1,9},{2,10},{3,11},{4,12},{5,13},{6,14},{7,15},{8,0},{9,1},... | collective-permute-start | bytes 73736 | tf_op jit(solution)/shard_map/ppermute | solution.py:54
  126.6 6.8 %collective-permute-start.6 = (f32[2]{0:T(128)S(1)}, f32[2]{0:T(128)S(1)}, u32[]{:S(2)}, u32[]{:S(2)}) collective-permute-start(f32[2]{0:T(128)S(1)} %pad_maximum_fusion.3), channel_id=1, source_target_pairs={{0,16},{16,32},{32,48},{48,64},{64,80},{80,96},{96,112},{112,0},{1... | collective-permute-start | bytes 32 | tf_op jit(solution)/shard_map/ppermute | solution.py:54
  134.7 1.6 %collective-permute-start.8 = (f32[2]{0:T(128)S(1)}, f32[2]{0:T(128)S(1)}, u32[]{:S(2)}, u32[]{:S(2)}) collective-permute-start(f32[2]{0:T(128)S(1)} %pad_maximum_fusion.3), channel_id=1, source_target_pairs={{0,48},{16,64},{32,80},{48,96},{64,112},{80,0},{96,16},{112,32},{1... | collective-permute-start | bytes 32 | tf_op jit(solution)/shard_map/ppermute | solution.py:54
  136.7 2.0 %collective-permute-start.10 = (f32[2]{0:T(128)S(1)}, f32[2]{0:T(128)S(1)}, u32[]{:S(2)}, u32[]{:S(2)}) collective-permute-start(f32[2]{0:T(128)S(1)} %pad_maximum_fusion.3), channel_id=1, source_target_pairs={{0,80},{16,96},{32,112},{48,0},{64,16},{80,32},{96,48},{112,64},{1... | collective-permute-start | bytes 32 | tf_op jit(solution)/shard_map/ppermute | solution.py:54
  141.0 1.5 %collective-permute-start.12 = (f32[2]{0:T(128)S(1)}, f32[2]{0:T(128)S(1)}, u32[]{:S(2)}, u32[]{:S(2)}) collective-permute-start(f32[2]{0:T(128)S(1)} %pad_maximum_fusion.3), channel_id=1, source_target_pairs={{0,112},{16,0},{32,16},{48,32},{64,48},{80,64},{96,80},{112,96},{1... | collective-permute-start | bytes 32 | tf_op jit(solution)/shard_map/ppermute | solution.py:54
  142.6 1.5 %collective-permute-done.12 = f32[2]{0:T(128)S(1)} collective-permute-done((f32[2]{0:T(128)S(1)}, f32[2]{0:T(128)S(1)}, u32[]{:S(2)}, u32[]{:S(2)}) %collective-permute-start.12) | collective-permute-done | bytes 40 | tf_op jit(solution)/shard_map/ppermute | solution.py:54
  (96 shorter events, 19.3 us)
Async XLA Ops:
  0.6 16.8 %copy-start.4 = (u32[128]{0:T(128)S(1)}, u32[128]{0:T(128)}, u32[]{:S(2)}) copy-start(u32[128]{0:T(128)} %constant.173) | copy-start | bytes 1540
  0.6 15.4 %copy-start = (s32[128]{0:T(128)S(1)}, s32[128]{0:T(128)}, u32[]{:S(2)}) copy-start(s32[128]{0:T(128)} %param.10) | copy-start | bytes 1540
  7.6 33.9 %all-to-all-start = ((bf16[16,32,1536]{2,1,0:T(8,128)(2,1)}), bf16[16,32,1536]{2,1,0:T(8,128)(2,1)S(1)}, u32[]{:S(2)}, u32[]{:S(2)}) async-start(bf16[16,32,1536]{2,1,0:T(8,128)(2,1)} %stack.190), calls=%async_computation | async-start | bytes 3145728 | tf_op jit(solution)/shard_map/all_to_all | solution.py:112
  42.7 25.1 %all-to-all-start.1 = ((bf16[16,32,1536]{2,1,0:T(8,128)(2,1)}), bf16[16,32,1536]{2,1,0:T(8,128)(2,1)S(1)}, u32[]{:S(2)}, u32[]{:S(2)}) async-start(bf16[16,32,1536]{2,1,0:T(8,128)(2,1)} %stack.196), calls=%async_computation.1 | async-start | bytes 3145728 | tf_op jit(solution)/shard_map/all_to_all | solution.py:112
  69.1 27.0 %all-to-all-start.2 = ((bf16[16,32,1536]{2,1,0:T(8,128)(2,1)}), bf16[16,32,1536]{2,1,0:T(8,128)(2,1)S(1)}, u32[]{:S(2)}, u32[]{:S(2)}) async-start(bf16[16,32,1536]{2,1,0:T(8,128)(2,1)} %stack.202), calls=%async_computation.2 | async-start | bytes 3145728 | tf_op jit(solution)/shard_map/all_to_all | solution.py:112
  112.1 4.0 %collective-permute-start = (f32[4,1536]{1,0:T(4,128)S(1)}, f32[4,1536]{1,0:T(4,128)S(1)}, u32[]{:S(2)}, u32[]{:S(2)}) collective-permute-start(f32[4,1536]{1,0:T(4,128)S(1)} %reshape.534), channel_id=1, source_target_pairs={{0,1},{1,2},{2,3},{3,0},{4,5},{5,6},{6,7},{7,4},{8,9},{9,10},{10,1... | collective-permute-start | bytes 73736 | tf_op jit(solution)/shard_map/ppermute | solution.py:54
  112.7 4.2 %collective-permute-start.1 = (f32[4,1536]{1,0:T(4,128)S(1)}, f32[4,1536]{1,0:T(4,128)S(1)}, u32[]{:S(2)}, u32[]{:S(2)}) collective-permute-start(f32[4,1536]{1,0:T(4,128)S(1)} %reshape.534), channel_id=1, source_target_pairs={{0,2},{1,3},{2,0},{3,1},{4,6},{5,7},{6,4},{7,5},{8,10},{9,11},{10,... | collective-permute-start | bytes 73736 | tf_op jit(solution)/shard_map/ppermute | solution.py:54
  114.4 2.7 %collective-permute-start.2 = (f32[4,1536]{1,0:T(4,128)S(1)}, f32[4,1536]{1,0:T(4,128)S(1)}, u32[]{:S(2)}, u32[]{:S(2)}) collective-permute-start(f32[4,1536]{1,0:T(4,128)S(1)} %reshape.534), channel_id=1, source_target_pairs={{0,3},{1,0},{2,1},{3,2},{4,7},{5,4},{6,5},{7,6},{8,11},{9,8},{10,9... | collective-permute-start | bytes 73736 | tf_op jit(solution)/shard_map/ppermute | solution.py:54
  118.0 5.4 %collective-permute-start.3 = (f32[4,1536]{1,0:T(4,128)S(1)}, f32[4,1536]{1,0:T(4,128)S(1)}, u32[]{:S(2)}, u32[]{:S(2)}) collective-permute-start(f32[4,1536]{1,0:T(4,128)S(1)} %get-tuple-element.104), channel_id=1, source_target_pairs={{0,4},{1,5},{2,6},{3,7},{4,8},{5,9},{6,10},{7,11},{8,12},{9,13},{1... | collective-permute-start | bytes 73736 | tf_op jit(solution)/shard_map/ppermute | solution.py:54
  120.1 4.2 %collective-permute-start.4 = (f32[4,1536]{1,0:T(4,128)S(1)}, f32[4,1536]{1,0:T(4,128)S(1)}, u32[]{:S(2)}, u32[]{:S(2)}) collective-permute-start(f32[4,1536]{1,0:T(4,128)S(1)} %get-tuple-element.104), channel_id=1, source_target_pairs={{0,8},{1,9},{2,10},{3,11},{4,12},{5,13},{6,14},{7,15},{8,0},{9,1},... | collective-permute-start | bytes 73736 | tf_op jit(solution)/shard_map/ppermute | solution.py:54
  121.7 2.7 %collective-permute-start.5 = (f32[4,1536]{1,0:T(4,128)S(1)}, f32[4,1536]{1,0:T(4,128)S(1)}, u32[]{:S(2)}, u32[]{:S(2)}) collective-permute-start(f32[4,1536]{1,0:T(4,128)S(1)} %get-tuple-element.104), channel_id=1, source_target_pairs={{0,12},{1,13},{2,14},{3,15},{4,0},{5,1},{6,2},{7,3},{8,4},{9,5},{1... | collective-permute-start | bytes 73736 | tf_op jit(solution)/shard_map/ppermute | solution.py:54
  126.6 13.5 %collective-permute-start.6 = (f32[2]{0:T(128)S(1)}, f32[2]{0:T(128)S(1)}, u32[]{:S(2)}, u32[]{:S(2)}) collective-permute-start(f32[2]{0:T(128)S(1)} %pad_maximum_fusion.3), channel_id=1, source_target_pairs={{0,16},{16,32},{32,48},{48,64},{64,80},{80,96},{96,112},{112,0},{1... | collective-permute-start | bytes 32 | tf_op jit(solution)/shard_map/ppermute | solution.py:54
  133.4 7.6 %collective-permute-start.7 = (f32[2]{0:T(128)S(1)}, f32[2]{0:T(128)S(1)}, u32[]{:S(2)}, u32[]{:S(2)}) collective-permute-start(f32[2]{0:T(128)S(1)} %pad_maximum_fusion.3), channel_id=1, source_target_pairs={{0,32},{16,48},{32,64},{48,80},{64,96},{80,112},{96,0},{112,16},{1... | collective-permute-start | bytes 32 | tf_op jit(solution)/shard_map/ppermute | solution.py:54
  134.7 7.8 %collective-permute-start.8 = (f32[2]{0:T(128)S(1)}, f32[2]{0:T(128)S(1)}, u32[]{:S(2)}, u32[]{:S(2)}) collective-permute-start(f32[2]{0:T(128)S(1)} %pad_maximum_fusion.3), channel_id=1, source_target_pairs={{0,48},{16,64},{32,80},{48,96},{64,112},{80,0},{96,16},{112,32},{1... | collective-permute-start | bytes 32 | tf_op jit(solution)/shard_map/ppermute | solution.py:54
  136.4 6.2 %collective-permute-start.9 = (f32[2]{0:T(128)S(1)}, f32[2]{0:T(128)S(1)}, u32[]{:S(2)}, u32[]{:S(2)}) collective-permute-start(f32[2]{0:T(128)S(1)} %pad_maximum_fusion.3), channel_id=1, source_target_pairs={{0,64},{16,80},{32,96},{48,112},{64,0},{80,16},{96,32},{112,48},{1... | collective-permute-start | bytes 32 | tf_op jit(solution)/shard_map/ppermute | solution.py:54
  136.7 5.9 %collective-permute-start.10 = (f32[2]{0:T(128)S(1)}, f32[2]{0:T(128)S(1)}, u32[]{:S(2)}, u32[]{:S(2)}) collective-permute-start(f32[2]{0:T(128)S(1)} %pad_maximum_fusion.3), channel_id=1, source_target_pairs={{0,80},{16,96},{32,112},{48,0},{64,16},{80,32},{96,48},{112,64},{1... | collective-permute-start | bytes 32 | tf_op jit(solution)/shard_map/ppermute | solution.py:54
  139.7 7.1 %copy-start.2 = (f32[128]{0:T(128)}, f32[128]{0:T(128)S(1)}, u32[]{:S(2)}) copy-start(f32[128]{0:T(128)S(1)} %fusion.41) | copy-start | bytes 1540
  139.9 6.8 %copy-start.3 = (f32[128]{0:T(128)}, f32[128]{0:T(128)S(1)}, u32[]{:S(2)}) copy-start(f32[128]{0:T(128)S(1)} %fusion.40) | copy-start | bytes 1540
  140.1 6.7 %copy-start.1 = (f32[128]{0:T(128)}, f32[128]{0:T(128)S(1)}, u32[]{:S(2)}) copy-start(f32[128]{0:T(128)S(1)} %select_dynamic-update-slice_fusion) | copy-start | bytes 1540
  140.1 2.5 %collective-permute-start.11 = (f32[2]{0:T(128)S(1)}, f32[2]{0:T(128)S(1)}, u32[]{:S(2)}, u32[]{:S(2)}) collective-permute-start(f32[2]{0:T(128)S(1)} %pad_maximum_fusion.3), channel_id=1, source_target_pairs={{0,96},{16,112},{32,0},{48,16},{64,32},{80,48},{96,64},{112,80},{1... | collective-permute-start | bytes 32 | tf_op jit(solution)/shard_map/ppermute | solution.py:54
  141.0 3.1 %collective-permute-start.12 = (f32[2]{0:T(128)S(1)}, f32[2]{0:T(128)S(1)}, u32[]{:S(2)}, u32[]{:S(2)}) collective-permute-start(f32[2]{0:T(128)S(1)} %pad_maximum_fusion.3), channel_id=1, source_target_pairs={{0,112},{16,0},{32,16},{48,32},{64,48},{80,64},{96,80},{112,96},{1... | collective-permute-start | bytes 32 | tf_op jit(solution)/shard_map/ppermute | solution.py:54
